TPU v7x, 256 devices: a whole 4x4x8 slice. The times are simulated.
256 devices in a mesh: row: 32 (over z, x), col: 8 (over y, core).
Axes of the slice: x: 4, y: 4, z: 8, core: 2. Of those that a mesh axis runs over, the one named last changes fastest.
Arguments:
- x_points: bfloat16 [32768, 64], P(('row', 'col')), may hold values from -6 to 6
- y_points: bfloat16 [65536, 64], P(('col', 'row')), may hold values from -6 to 6
- row_mass: bfloat16 [32768], P(('row', 'col')), may hold values from 1 to 30, as said below
- col_mass: bfloat16 [65536], P(('col', 'row')), may hold values from 1 to 30, as said below
- multipliers: bfloat16 [32768, 64], P(('row', 'col')), may hold values from -12 to 12
- col_potential: bfloat16 [65536], P(('col', 'row')), may hold values from -3 to 3
- basket: float32 [64], replicated, may hold values from 0.05 to 0.25
- damping: float32 [64], replicated, may hold values from 0.3 to 1.5
Outputs:
- row_potential: float32 [32768], P('row')
- col_potential_new: float32 [65536], P('col')
- multipliers_new: float32 [32768, 64], P(('row', 'col'))
Inputs may be any that keep to these rules, and one draw needn't show every extreme that they name: `row_mass`: weights rise along the points' order by up to a factor of three. `col_mass`: weights rise along the points' order by up to a factor of three.
All inputs are finite; a program needn't handle non-finite values.
Results may differ from a plain program's by a relative error of at most 0.0012.
Values may be sent and summed in bfloat16 or wider, within the bound.
No kernel may reach another device: no remote copies, remote signals or barrier semaphores. Data moves between devices by JAX's collectives and lax.ppermute only.
A program may use at most 64 MiB of HBM per device.

v0:
```python
import jax
import jax.numpy as jnp
from jax import lax
from jax.sharding import PartitionSpec as P

EPS = 0.5
KAPPA = 0.5
RIDGE = 1.0


def joined(value, axis, join):
    pieces = jax.tree.map(lambda part: lax.all_gather(part, axis), value)
    head = jax.tree.map(lambda part: part[0], pieces)
    tail = jax.tree.map(lambda part: part[1:], pieces)
    subtotal, _ = lax.scan(lambda subtotal, piece: (join(subtotal, piece), None), head, tail)
    return subtotal


def prepare_rows(x_rows, mult_rows, basket):
    xf = x_rows.astype(jnp.float32)
    hf = mult_rows.astype(jnp.float32)
    width = xf.shape[1]
    query = hf + 2.0 * KAPPA / width * xf
    row_term = -jnp.sum(hf * xf, axis=1) - KAPPA / width * jnp.sum(xf * xf, axis=1)
    row_basket = jnp.sum(xf * basket[None, :], axis=1)
    return (query, row_term, row_basket)


def prepare_cols(y_cols, basket):
    yf = y_cols.astype(jnp.float32)
    width = yf.shape[1]
    col_term = -(KAPPA / width) * jnp.sum(yf * yf, axis=1)
    col_basket = jnp.sum(yf * basket[None, :], axis=1)
    features = jnp.concatenate([yf, yf * yf], axis=1).astype(jnp.bfloat16)
    return (yf, col_term, col_basket, features)


def scores(query, row_term, row_basket, y_float, col_term, col_basket):
    dots = lax.dot_general(
        query,
        y_float,
        (((1,), (1,)), ((), ())),
        precision=lax.Precision.HIGHEST,
        preferred_element_type=jnp.float32,
    )
    payoff = jax.nn.relu(col_basket[None, :] - row_basket[:, None])
    return (dots + row_term[:, None] + col_term[None, :] + payoff) / EPS


def lse_join(first, second):
    top = jnp.maximum(first[0], second[0])
    total = first[1] * jnp.exp(first[0] - top) + second[1] * jnp.exp(second[0] - top)
    return (top, total)


def on_device(x_points, y_points, row_mass, col_mass, multipliers, col_potential, basket, damping):
    x_rows, mult_rows, mass_rows = (
        lax.all_gather(x_points, "col", axis=0, tiled=True),
        lax.all_gather(multipliers, "col", axis=0, tiled=True),
        lax.all_gather(row_mass, "col", axis=0, tiled=True),
    )
    y_cols, pot_cols, mass_cols = (
        lax.all_gather(y_points, "row", axis=0, tiled=True),
        lax.all_gather(col_potential, "row", axis=0, tiled=True),
        lax.all_gather(col_mass, "row", axis=0, tiled=True),
    )
    query, row_term, row_basket = prepare_rows(x_rows, mult_rows, basket)
    y_float, col_term, col_basket, features = prepare_cols(y_cols, basket)
    row_weight = mass_rows.astype(jnp.float32)
    col_weight = mass_cols.astype(jnp.float32)
    log_row = jnp.log(row_weight)
    log_col = jnp.log(col_weight)
    nrows = x_rows.shape[0]
    block = min(128, nrows)
    count = nrows // block
    starts = jnp.arange(count, dtype=jnp.int32) * block

    def cut(arr, start):
        return lax.dynamic_slice_in_dim(arr, start, block, 0)

    def block_scores(start):
        return scores(
            cut(query, start),
            cut(row_term, start),
            cut(row_basket, start),
            y_float,
            col_term,
            col_basket,
        )

    gshift = pot_cols.astype(jnp.float32) / EPS + log_col

    def row_pass(start):
        z = block_scores(start) + gshift[None, :]
        top = jnp.max(z, axis=1)
        total = jnp.sum(jnp.exp(z - top[:, None]), axis=1)
        return (top, total)

    row_tops, row_totals = lax.map(row_pass, starts)
    row_tops = row_tops.reshape(nrows)
    row_totals = row_totals.reshape(nrows)
    mu_total, nu_total = lax.psum(
        (jnp.sum(row_mass.astype(jnp.float32)), jnp.sum(col_mass.astype(jnp.float32))),
        ("row", "col"),
    )
    row_top, row_total = joined((row_tops, row_totals), "col", lse_join)
    log_nu_total = jnp.log(nu_total)
    row_potential = -EPS * (row_top + jnp.log(row_total) - log_nu_total)
    fshift = row_potential / EPS + log_row

    def col_pass(start):
        z = block_scores(start) + cut(fshift, start)[:, None]
        top = jnp.max(z, axis=0)
        total = jnp.sum(jnp.exp(z - top[None, :]), axis=0)
        return (top, total)

    col_tops, col_totals = lax.map(col_pass, starts)
    col_top = jnp.max(col_tops, axis=0)
    col_total = jnp.sum(col_totals * jnp.exp(col_tops - col_top[None, :]), axis=0)
    peak = lax.pmax(col_top, "row")
    scaled = col_total * jnp.exp(col_top - peak)
    whole = lax.psum(scaled, "row")
    col_potential_new = -EPS * (peak + jnp.log(whole) - jnp.log(mu_total))
    gq = col_potential_new / EPS + log_col - log_nu_total
    fq = row_potential / EPS

    def moment_pass(start):
        plan = jnp.exp(block_scores(start) + cut(fq, start)[:, None] + gq[None, :]).astype(
            jnp.bfloat16
        )
        both = jnp.dot(plan, features, preferred_element_type=jnp.float32)
        mass = jnp.sum(plan.astype(jnp.float32), axis=1)
        return (both, mass)

    both, mass = lax.map(moment_pass, starts)
    both = both.reshape(nrows, features.shape[1])
    mass = mass.reshape(nrows)
    share = x_points.shape[0]
    both_all, mass_all = lax.psum((both, mass), "col")
    offset = lax.axis_index("col") * share
    own_both = lax.dynamic_slice_in_dim(both_all, offset, share, 0)
    own_mass = lax.dynamic_slice_in_dim(mass_all, offset, share, 0)
    width = x_points.shape[1]
    first = own_both[:, :width]
    second = own_both[:, width:]
    xf = x_points.astype(jnp.float32)
    grad = first - xf * own_mass[:, None]
    curv = (second - 2.0 * xf * first + xf * xf * own_mass[:, None]) / EPS + RIDGE
    multipliers_new = multipliers.astype(jnp.float32) - damping[None, :] * grad / curv
    return (row_potential, col_potential_new, multipliers_new)


def solution(mesh):
    placed = (
        P(("row", "col"), None),
        P(("col", "row"), None),
        P(("row", "col")),
        P(("col", "row")),
        P(("row", "col"), None),
        P(("col", "row")),
        P(),
        P(),
    )
    return jax.shard_map(
        on_device,
        mesh=mesh,
        in_specs=placed,
        out_specs=(P("row"), P("col"), P(("row", "col"), None)),
        check_vma=False,
    )
```

profile of v0, /device:TPU:2, one launch (start us, length us, event | category | flops | bytes accessed | tf_op | source)
XLA Modules:
  0.0 851.1 jit_solution(13461661143674850518)
XLA Ops:
  11.3 79.4 %all-reduce = (f32[]{:T(128)}, f32[]{:T(128)}) all-reduce(f32[]{:T(128)} %convert_reduce_fusion.1, f32[]{:T(128)} %convert_reduce_fusion.2), channel_id=1, replica_groups=mesh['row'=32,'col'=8] {'row','col'}, use_global_device_ids=true, to_apply=%region_12.13 | all-reduce | flops 2 | bytes 16 | tf_op jit(solution)/shard_map/psum | solution.py:102
  95.0 42.6 %all-gather.1 = bf16[32,1,256]{2,1,0:T(2,128)(2,1)S(1)} all-gather(bf16[1,1,256]{2,1,0:T(2,128)(2,1)S(1)} %reshape.38), channel_id=1, replica_groups=mesh['row'=32,'col'=8] {'row'}, dimensions={0}, use_global_device_ids=true | all-gather | bytes 16896 | tf_op jit(solution)/shard_map/all_gather | solution.py:65
  137.6 40.5 %all-gather = bf16[32,1,256]{2,1,0:T(2,128)(2,1)S(1)} all-gather(bf16[1,1,256]{2,1,0:T(2,128)(2,1)S(1)} %reshape.36), channel_id=1, replica_groups=mesh['row'=32,'col'=8] {'row'}, dimensions={0}, use_global_device_ids=true | all-gather | bytes 16896 | tf_op jit(solution)/shard_map/all_gather | solution.py:64
  178.2 9.2 %all-gather.4 = bf16[8,1,128]{2,1,0:T(2,128)(2,1)S(1)} all-gather(bf16[1,1,128]{2,1,0:T(2,128)(2,1)} %bitcast.86), channel_id=1, replica_groups=mesh['row'=32,'col'=8] {'col'}, dimensions={0}, use_global_device_ids=true | all-gather | bytes 2304 | tf_op jit(solution)/shard_map/all_gather | solution.py:60
  187.4 12.8 %all_gather.24 = bf16[1024,64]{1,0:T(8,128)(2,1)S(1)} all-gather(bf16[128,64]{1,0:T(8,128)(2,1)S(1)} %copy.15), channel_id=1, replica_groups=mesh['row'=32,'col'=8] {'col'}, dimensions={0}, use_global_device_ids=true | all-gather | bytes 147456 | tf_op jit(solution)/shard_map/all_gather | solution.py:59
  200.2 12.8 %all_gather.25 = bf16[1024,64]{1,0:T(8,128)(2,1)S(1)} all-gather(bf16[128,64]{1,0:T(8,128)(2,1)S(1)} %copy.16), channel_id=1, replica_groups=mesh['row'=32,'col'=8] {'col'}, dimensions={0}, use_global_device_ids=true | all-gather | bytes 147456 | tf_op jit(solution)/shard_map/all_gather | solution.py:58
  221.7 80.0 %while.48 = (s32[]{:T(128)}, f32[8,128]{1,0:T(8,128)S(1)}, f32[8,128]{1,0:T(8,128)S(1)}, s32[8]{0:T(128)S(1)}, f32[1024,64]{1,0:T(8,128)S(1)}, /*index=5*/f32[81...) while((s32[]{:T(128)}, f32[8,128]{1,0:T(8,128)S(1)}, ...), condition=%wide.region_8.9_spmd, body=%wide.region_5.8_spmd.sunk | while | flops 815791872 | bytes 10656463 | solution.py:99
  224.4 6.5 fusion.52
  234.4 6.5 fusion.52
  244.4 6.5 fusion.52
  254.4 6.5 fusion.52
  264.4 6.5 fusion.52
  274.4 6.5 fusion.52
  284.4 6.5 fusion.52
  294.4 6.5 fusion.52
  301.7 12.9 %all-gather.2 = f32[8,1,1024]{2,1,0:T(1,128)S(1)} all-gather(f32[1,1,1024]{2,1,0:T(1,128)S(1)} %bitcast.83), channel_id=1, replica_groups=mesh['row'=32,'col'=8] {'col'}, dimensions={0}, use_global_device_ids=true | all-gather | bytes 36864 | tf_op jit(solution)/shard_map/all_gather | solution.py:12
  314.7 13.1 %all-gather.3 = f32[8,1,1024]{2,1,0:T(1,128)S(1)} all-gather(f32[1,1,1024]{2,1,0:T(1,128)S(1)} %bitcast.82), channel_id=1, replica_groups=mesh['row'=32,'col'=8] {'col'}, dimensions={0}, use_global_device_ids=true | all-gather | bytes 36864 | tf_op jit(solution)/shard_map/all_gather | solution.py:12
  328.7 80.8 %while.50 = (s32[]{:T(128)}, f32[8,8192]{1,0:T(8,128)S(1)}, f32[8,8192]{1,0:T(8,128)S(1)}, s32[8]{0:T(128)S(1)}, f32[1024,64]{1,0:T(8,128)S(1)}, /*index=5*/f32[...) while((s32[]{:T(128)}, f32[8,8192]{1,0:T(8,128)S(1)}, ...), condition=%wide.region_16.17_spmd, body=%wide.region_13.16_spmd.sunk | while | flops 815775744 | bytes 10851027 | solution.py:117
  331.5 6.4 fusion.54
  409.7 136.0 %pmax.7 = f32[8192]{0:T(1024)S(1)} all-reduce(f32[8192]{0:T(1024)S(1)} %reduce_max.27), channel_id=1, replica_groups=mesh['row'=32,'col'=8] {'row'}, use_global_device_ids=true, to_apply=%region_18.19 | all-reduce | flops 8192 | bytes 65536 | tf_op jit(solution)/shard_map/pmax | solution.py:120
  545.8 139.9 %psum.36 = f32[8192]{0:T(1024)S(1)} all-reduce(f32[8192]{0:T(1024)S(1)} %exponential_multiply_fusion), channel_id=1, replica_groups=mesh['row'=32,'col'=8] {'row'}, use_global_device_ids=true, to_apply=%region_20.21 | all-reduce | flops 8192 | bytes 65536 | tf_op jit(solution)/shard_map/psum | solution.py:122
  689.8 88.4 %while.51 = (s32[]{:T(128)}, f32[8,128,128]{2,1,0:T(8,128)S(1)}, f32[8,128]{1,0:T(8,128)S(1)}, s32[8]{0:T(128)S(1)}, f32[1024,64]{1,0:T(8,128)S(1)}, /*index=5*/...) while((s32[]{:T(128)}, f32[8,128,128]{2,1,0:T(8,128)S(1)}, ...), condition=%wide.region_25.26_spmd, body=%wide.region_23.25_spmd.sunk | while | flops 1085276032 | bytes 8624355 | solution.py:135
  692.5 7.5 convert_reduce_fusion.4
  703.6 7.5 convert_reduce_fusion.4
  714.6 7.5 convert_reduce_fusion.4
  725.7 7.5 convert_reduce_fusion.4
  736.7 7.5 convert_reduce_fusion.4
  747.8 7.5 convert_reduce_fusion.4
  758.8 7.5 convert_reduce_fusion.4
  769.9 7.5 convert_reduce_fusion.4
  779.2 12.4 %psum.39 = f32[1024]{0:T(1024)S(1)} all-reduce(f32[1024]{0:T(1024)S(1)} %bitcast.84), channel_id=1, replica_groups=mesh['row'=32,'col'=8] {'col'}, use_global_device_ids=true, to_apply=%region_27.28 | all-reduce | flops 1024 | bytes 8192 | tf_op jit(solution)/shard_map/psum | solution.py:139
  791.7 51.1 %all-reduce.3.cloned.1.call-done = f32[1024,128]{0,1:T(8,128)} async-done(((f32[1024,128]{0,1:T(8,128)}), f32[1024,128]{0,1:T(8,128)}) %all-reduce.3.cloned.1.call-update) | async-done | bytes 524304 | tf_op jit(solution)/shard_map/psum | solution.py:139
  (225 shorter events, 107.6 us)
Async XLA Ops:
  7.2 207.1 %all-gather.7.cloned.1.call-start = ((), (), s32[]{:S(2)}) async-start(), calls=%async_computation | async-start | bytes 2162688 | tf_op jit(solution)/shard_map/all_gather | solution.py:63
  8.7 834.1 %all-reduce.3.cloned.1.call-start = ((), (), s32[]{:S(2)}) async-start(), calls=%async_computation.1 | async-start | bytes 1048576 | tf_op jit(solution)/shard_map/psum | solution.py:139
  214.3 5.2 copy-start
  689.7 153.1 %copy-start.1 = (bf16[128,64]{0,1:T(8,128)(2,1)S(1)}, bf16[128,64]{0,1:T(8,128)(2,1)}, u32[]{:S(2)}) copy-start(bf16[128,64]{0,1:T(8,128)(2,1)} %param.16) | copy-start | bytes 49156
  689.7 153.1 %copy-start.2 = (bf16[128,64]{0,1:T(8,128)(2,1)S(1)}, bf16[128,64]{0,1:T(8,128)(2,1)}, u32[]{:S(2)}) copy-start(bf16[128,64]{0,1:T(8,128)(2,1)} %param.20) | copy-start | bytes 49156
  689.8 153.1 %copy-start.3 = (f32[64]{0:T(128)S(1)}, f32[64]{0:T(128)}, u32[]{:S(2)}) copy-start(f32[64]{0:T(128)} %param.23) | copy-start | bytes 772
Sparse Core Ops, SparseCore 0:
  10.6 79.5 all-gather.6
  779.3 63.4 all-reduce.2
where the time goes:
time: 853 us; the launch traced here: 851 us
  blocking collectives  512 us (60%)
  matrix products  169 us (20%)
  waiting for transfers between devices  51.2 us (6%)
  loops' own time  47.5 us (6%)
  other arithmetic  28.6 us (3%)
  local copies, waits for them, and re-layouts  27.8 us (3%)
  between operations  15.6 us (2%)
    dot_general x24, matrix products, scores(): lax.dot_general(query, y_float, (((1,), (1,)), ((), ())), precision=lax.P...  163 us
    psum x1, blocking collectives, on_device(): whole = lax.psum(scaled, 'row')  140 us
    pmax x1, blocking collectives, on_device(): peak = lax.pmax(col_top, 'row')  136 us
    psum x1, blocking collectives, on_device(): lax.psum((jnp.sum(row_mass.astype(jnp.float32)), jnp.sum(col_mass.astype(...  79.4 us
    psum x1, waiting for transfers between devices, on_device(): both_all, mass_all = lax.psum((both, mass), 'col')  51.1 us
    all_gather x1, blocking collectives, on_device(): lax.all_gather(col_mass, 'row', axis=0, tiled=True)  42.6 us
    all_gather x1, blocking collectives, on_device(): lax.all_gather(col_potential, 'row', axis=0, tiled=True)  40.5 us
    all_gather x2, blocking collectives, joined(): pieces = jax.tree.map(lambda part: lax.all_gather(part, axis), value)  26 us
  transfers between devices with their start and end apart: 2, of which 1 were waited for; matrix products, arithmetic and copies ran while one was open for 1% of the time, Pallas kernels for 0%

commit v1 on v0

--- a/solution.py
+++ b/solution.py
@@ -119,7 +119,7 @@
     col_total = jnp.sum(col_totals * jnp.exp(col_tops - col_top[None, :]), axis=0)
     peak = lax.pmax(col_top, "row")
     scaled = col_total * jnp.exp(col_top - peak)
-    whole = lax.psum(scaled, "row")
+    whole = jnp.sum(lax.all_gather(scaled, "row"), axis=0)
     col_potential_new = -EPS * (peak + jnp.log(whole) - jnp.log(mu_total))
     gq = col_potential_new / EPS + log_col - log_nu_total
     fq = row_potential / EPS

time: 853 us -> 792 us (0.928)
  blocking collectives: 512 us -> 372 us
  waiting for transfers between devices: 51.2 us -> 123 us
    psum x1 -> x0, blocking collectives: 140 us -> none  [on_device(): whole = lax.psum(scaled, 'row')]
    all_gather x0 -> x1, waiting for transfers between devices: none -> 70.8 us  [on_device(): whole = jnp.sum(lax.all_gather(scaled, 'row'), axis=0)]
  transfers between devices with their start and end apart: 2 -> 3, of which waited for: 1 -> 2; matrix products, arithmetic and copies ran while one was open for 1% -> 1% of each run, Pallas kernels for 0% -> 0%
where the time goes in v1:
time: 792 us; the launch traced here: 791 us
  blocking collectives  372 us (47%)
  matrix products  174 us (22%)
  waiting for transfers between devices  123 us (16%)
  loops' own time  47.4 us (6%)
  local copies, waits for them, and re-layouts  30.2 us (4%)
  other arithmetic  29.3 us (4%)
  between operations  15.3 us (2%)
    dot_general x24, matrix products, scores(): lax.dot_general(query, y_float, (((1,), (1,)), ((), ())), precision=lax.P...  163 us
    pmax x1, blocking collectives, on_device(): peak = lax.pmax(col_top, 'row')  136 us
    psum x1, blocking collectives, on_device(): lax.psum((jnp.sum(row_mass.astype(jnp.float32)), jnp.sum(col_mass.astype(...  79.4 us
    all_gather x1, waiting for transfers between devices, on_device(): whole = jnp.sum(lax.all_gather(scaled, 'row'), axis=0)  70.8 us
    psum x1, waiting for transfers between devices, on_device(): both_all, mass_all = lax.psum((both, mass), 'col')  52.5 us
    all_gather x1, blocking collectives, on_device(): lax.all_gather(col_mass, 'row', axis=0, tiled=True)  42.5 us
    all_gather x1, blocking collectives, on_device(): lax.all_gather(col_potential, 'row', axis=0, tiled=True)  40.6 us
    all_gather x2, blocking collectives, joined(): pieces = jax.tree.map(lambda part: lax.all_gather(part, axis), value)  26 us
  transfers between devices with their start and end apart: 3, of which 2 were waited for; matrix products, arithmetic and copies ran while one was open for 1% of the time, Pallas kernels for 0%

profile of v1, /device:TPU:2, one launch (start us, length us, event | category | flops | bytes accessed | tf_op | source)
XLA Modules:
  0.0 790.8 jit_solution(12919937706743794005)
XLA Ops:
  11.3 79.4 %all-reduce = (f32[]{:T(128)}, f32[]{:T(128)}) all-reduce(f32[]{:T(128)} %convert_reduce_fusion.1, f32[]{:T(128)} %convert_reduce_fusion.2), channel_id=1, replica_groups=mesh['row'=32,'col'=8] {'row','col'}, use_global_device_ids=true, to_apply=%region_12.13 | all-reduce | flops 2 | bytes 16 | tf_op jit(solution)/shard_map/psum | solution.py:102
  94.3 42.5 %all-gather.2 = bf16[32,1,256]{2,1,0:T(2,128)(2,1)S(1)} all-gather(bf16[1,1,256]{2,1,0:T(2,128)(2,1)S(1)} %reshape.39), channel_id=1, replica_groups=mesh['row'=32,'col'=8] {'row'}, dimensions={0}, use_global_device_ids=true | all-gather | bytes 16896 | tf_op jit(solution)/shard_map/all_gather | solution.py:65
  136.8 40.6 %all-gather.1 = bf16[32,1,256]{2,1,0:T(2,128)(2,1)S(1)} all-gather(bf16[1,1,256]{2,1,0:T(2,128)(2,1)S(1)} %reshape.37), channel_id=1, replica_groups=mesh['row'=32,'col'=8] {'row'}, dimensions={0}, use_global_device_ids=true | all-gather | bytes 16896 | tf_op jit(solution)/shard_map/all_gather | solution.py:64
  177.5 9.2 %all-gather.5 = bf16[8,1,128]{2,1,0:T(2,128)(2,1)S(1)} all-gather(bf16[1,1,128]{2,1,0:T(2,128)(2,1)} %bitcast.86), channel_id=1, replica_groups=mesh['row'=32,'col'=8] {'col'}, dimensions={0}, use_global_device_ids=true | all-gather | bytes 2304 | tf_op jit(solution)/shard_map/all_gather | solution.py:60
  186.7 12.8 %all_gather.30 = bf16[1024,64]{1,0:T(8,128)(2,1)S(1)} all-gather(bf16[128,64]{1,0:T(8,128)(2,1)S(1)} %copy.19), channel_id=1, replica_groups=mesh['row'=32,'col'=8] {'col'}, dimensions={0}, use_global_device_ids=true | all-gather | bytes 147456 | tf_op jit(solution)/shard_map/all_gather | solution.py:59
  199.5 12.8 %all_gather.31 = bf16[1024,64]{1,0:T(8,128)(2,1)S(1)} all-gather(bf16[128,64]{1,0:T(8,128)(2,1)S(1)} %copy.20), channel_id=1, replica_groups=mesh['row'=32,'col'=8] {'col'}, dimensions={0}, use_global_device_ids=true | all-gather | bytes 147456 | tf_op jit(solution)/shard_map/all_gather | solution.py:58
  221.0 80.0 %while.48 = (s32[]{:T(128)}, f32[8,128]{1,0:T(8,128)S(1)}, f32[8,128]{1,0:T(8,128)S(1)}, s32[8]{0:T(128)S(1)}, f32[1024,64]{1,0:T(8,128)S(1)}, /*index=5*/f32[81...) while((s32[]{:T(128)}, f32[8,128]{1,0:T(8,128)S(1)}, ...), condition=%wide.region_8.9_spmd, body=%wide.region_5.8_spmd.sunk | while | flops 815791872 | bytes 10656463 | solution.py:99
  223.7 6.5 fusion.52
  233.7 6.5 fusion.52
  243.7 6.5 fusion.52
  253.7 6.5 fusion.52
  263.7 6.5 fusion.52
  273.7 6.5 fusion.52
  283.7 6.5 fusion.52
  293.7 6.5 fusion.52
  301.0 12.9 %all-gather.3 = f32[8,1,1024]{2,1,0:T(1,128)S(1)} all-gather(f32[1,1,1024]{2,1,0:T(1,128)S(1)} %bitcast.83), channel_id=1, replica_groups=mesh['row'=32,'col'=8] {'col'}, dimensions={0}, use_global_device_ids=true | all-gather | bytes 36864 | tf_op jit(solution)/shard_map/all_gather | solution.py:12
  313.9 13.1 %all-gather.4 = f32[8,1,1024]{2,1,0:T(1,128)S(1)} all-gather(f32[1,1,1024]{2,1,0:T(1,128)S(1)} %bitcast.82), channel_id=1, replica_groups=mesh['row'=32,'col'=8] {'col'}, dimensions={0}, use_global_device_ids=true | all-gather | bytes 36864 | tf_op jit(solution)/shard_map/all_gather | solution.py:12
  328.0 80.8 %while.50 = (s32[]{:T(128)}, f32[8,8192]{1,0:T(8,128)S(1)}, f32[8,8192]{1,0:T(8,128)S(1)}, s32[8]{0:T(128)S(1)}, f32[1024,64]{1,0:T(8,128)S(1)}, /*index=5*/f32[...) while((s32[]{:T(128)}, f32[8,8192]{1,0:T(8,128)S(1)}, ...), condition=%wide.region_16.17_spmd, body=%wide.region_13.16_spmd.sunk | while | flops 815775744 | bytes 10851027 | solution.py:117
  340.8 6.4 fusion.54
  408.9 136.0 %pmax.7 = f32[8192]{0:T(1024)S(1)} all-reduce(f32[8192]{0:T(1024)S(1)} %reduce_max.27), channel_id=1, replica_groups=mesh['row'=32,'col'=8] {'row'}, use_global_device_ids=true, to_apply=%region_18.19 | all-reduce | flops 8192 | bytes 65536 | tf_op jit(solution)/shard_map/pmax | solution.py:120
  549.8 70.8 %all-gather.11.cloned.1.call-done = f32[262144]{0:T(1024)} async-done(((f32[8192]{0:T(1024)}), f32[262144]{0:T(1024)}) %all-gather.11.cloned.1.call-update) | async-done | bytes 1048592 | tf_op jit(solution)/shard_map/all_gather | solution.py:122
  622.8 93.0 %while.51 = (s32[]{:T(128)}, f32[8,128,128]{2,1,0:T(8,128)}, f32[8,128]{1,0:T(8,128)S(1)}, s32[8]{0:T(128)S(1)}, f32[1024,64]{1,0:T(8,128)}, /*index=5*/f32[8192...) while((s32[]{:T(128)}, f32[8,128,128]{2,1,0:T(8,128)}, ...), condition=%wide.region_25.26_spmd, body=%wide.region_23.25_spmd.sunk | while | flops 1085276032 | bytes 10721507 | solution.py:135
  625.5 7.5 convert_reduce_fusion.4
  637.2 7.5 convert_reduce_fusion.4
  648.8 7.5 convert_reduce_fusion.4
  660.4 7.5 convert_reduce_fusion.4
  672.0 7.5 convert_reduce_fusion.4
  683.6 7.5 convert_reduce_fusion.4
  695.3 7.5 convert_reduce_fusion.4
  706.9 7.5 convert_reduce_fusion.4
  717.8 12.4 %psum.31 = f32[1024]{0:T(1024)S(1)} all-reduce(f32[1024]{0:T(1024)S(1)} %bitcast.84), channel_id=1, replica_groups=mesh['row'=32,'col'=8] {'col'}, use_global_device_ids=true, to_apply=%region_27.28 | all-reduce | flops 1024 | bytes 8192 | tf_op jit(solution)/shard_map/psum | solution.py:139
  730.3 52.5 %all-reduce.3.cloned.1.call-done = f32[1024,128]{0,1:T(8,128)} async-done(((f32[1024,128]{0,1:T(8,128)}), f32[1024,128]{0,1:T(8,128)}) %all-reduce.3.cloned.1.call-update) | async-done | bytes 524304 | tf_op jit(solution)/shard_map/psum | solution.py:139
  (231 shorter events, 115.3 us)
Async XLA Ops:
  7.2 206.4 %all-gather.9.cloned.1.call-start = ((), (), s32[]{:S(2)}) async-start(), calls=%async_computation | async-start | bytes 2162688 | tf_op jit(solution)/shard_map/all_gather | solution.py:63
  8.7 611.9 %all-gather.11.cloned.1.call-start = ((), (), s32[]{:S(2)}) async-start(), calls=%async_computation.2 | async-start | bytes 1081344 | tf_op jit(solution)/shard_map/all_gather | solution.py:122
  213.6 5.2 copy-start
  408.8 137.6 %copy-start.1 = (f32[1024,64]{1,0:T(8,128)}, f32[1024,64]{1,0:T(8,128)S(1)}, u32[]{:S(2)}) copy-start(f32[1024,64]{1,0:T(8,128)S(1)} %get-tuple-element.751) | copy-start | bytes 786436
  545.6 237.2 %all-reduce.3.cloned.1.call-start = ((), (), s32[]{:S(2)}) async-start(), calls=%async_computation.1 | async-start | bytes 1048576 | tf_op jit(solution)/shard_map/psum | solution.py:139
  622.8 160.1 %copy-start.2 = (bf16[128,64]{0,1:T(8,128)(2,1)S(1)}, bf16[128,64]{0,1:T(8,128)(2,1)}, u32[]{:S(2)}) copy-start(bf16[128,64]{0,1:T(8,128)(2,1)} %param.16) | copy-start | bytes 49156
  622.8 160.1 %copy-start.3 = (bf16[128,64]{0,1:T(8,128)(2,1)S(1)}, bf16[128,64]{0,1:T(8,128)(2,1)}, u32[]{:S(2)}) copy-start(bf16[128,64]{0,1:T(8,128)(2,1)} %param.20) | copy-start | bytes 49156
  622.8 160.1 %copy-start.4 = (f32[64]{0:T(128)S(1)}, f32[64]{0:T(128)}, u32[]{:S(2)}) copy-start(f32[64]{0:T(128)} %param.23) | copy-start | bytes 772
Sparse Core Ops, SparseCore 0:
  10.6 79.5 all-gather.8
  545.8 74.7 all-gather.10
  717.9 64.8 all-reduce.2
